TPU v7x, 512 devices: a whole 4x4x16 slice. The times are simulated.
512 devices in a mesh: band: 32 (over x, z_lo), grid: 16 (over z_hi, y, core).
Axes of the slice: x: 4, y: 4, z: 16 (z_hi: 2, z_lo: 8; z = z_hi * 8 + z_lo), core: 2. Of those that a mesh axis runs over, the one named last changes fastest.
Arguments:
- trial_bands: float32 [64, 160, 32, 128], P('band', 'grid'), may hold values from -6 to 6
- potential: float32 [160, 32, 128], P('grid'), may hold values from -2 to 0
Outputs:
- filtered: float32 [64, 160, 32, 128], P('band', 'grid')
- projected: float32 [64, 64], P('band')
- residual_norms: float32 [64], P('band')
All inputs are finite; a program needn't handle non-finite values.
Results may differ from a plain program's by a relative error of at most 0.00016.
Values sent between devices are 32-bit elements; how exact they have to be, the bound alone decides.
No kernel may reach another device: no remote copies, remote signals or barrier semaphores. Data moves between devices by JAX's collectives and lax.ppermute only.
A program may use at most 64 MiB of HBM per device.

v0:
```python
import jax
import jax.numpy as jnp
from jax import lax
from jax.sharding import PartitionSpec as P

CENTER = 4.25
HALF_WIDTH = 3.75
LOWEST = -2.0
SIGMA_ONE = HALF_WIDTH / (LOWEST - CENTER)
FOUR_THIRDS = 4.0 / 3.0
TWELFTH = 1.0 / 12.0
filter_degree = 4


def padded_2(cells, sides, width):
    for axis, dim in sides:
        count = lax.axis_size(axis)
        head = lax.slice_in_dim(cells, 0, width, axis=dim)
        tail = lax.slice_in_dim(cells, cells.shape[dim] - width, cells.shape[dim], axis=dim)
        cells = jnp.concatenate(
            [
                lax.ppermute(tail, axis, [(i, (i + 1) % count) for i in range(count)]),
                cells,
                lax.ppermute(head, axis, [((i + 1) % count, i) for i in range(count)]),
            ],
            axis=dim,
        )
    return cells


def operate(field_in, potential):
    padded = padded_2(field_in, (("grid", 1),), 2)
    plane_count = field_in.shape[1]
    near_sum = padded[:, 1 : 1 + plane_count] + padded[:, 3 : 3 + plane_count]
    near_sum = near_sum + jnp.roll(field_in, 1, 2) + jnp.roll(field_in, -1, 2)
    near_sum = near_sum + jnp.roll(field_in, 1, 3) + jnp.roll(field_in, -1, 3)
    far_sum = padded[:, 0:plane_count] + padded[:, 4 : 4 + plane_count]
    far_sum = far_sum + jnp.roll(field_in, 2, 2) + jnp.roll(field_in, -2, 2)
    far_sum = far_sum + jnp.roll(field_in, 2, 3) + jnp.roll(field_in, -2, 3)
    kinetic = 0.5 * (7.5 * field_in - FOUR_THIRDS * near_sum + TWELFTH * far_sum)
    return kinetic + potential * field_in


def on_device(trial_bands, potential):
    sigma_now = SIGMA_ONE
    previous = trial_bands
    current = (operate(trial_bands, potential) - CENTER * trial_bands) * (SIGMA_ONE / HALF_WIDTH)
    for repeat_index in range(filter_degree - 1):
        sigma_next = 1.0 / (2.0 / SIGMA_ONE - sigma_now)
        following = (operate(current, potential) - CENTER * current) * (
            2.0 * sigma_next / HALF_WIDTH
        ) - sigma_now * sigma_next * previous
        previous, current, sigma_now = (current, following, sigma_next)
    applied = operate(current, potential)
    band_count = current.shape[0]
    band_devices = lax.axis_size("band")
    total_bands = band_count * band_devices
    cell_count = current.shape[1] * current.shape[2] * current.shape[3]
    cell_total = cell_count * lax.axis_size("grid")
    inverse_cells = 1.0 / cell_total
    first_band = lax.axis_index("band") * band_count
    both = jnp.stack(
        [current.reshape(band_count, cell_count), applied.reshape(band_count, cell_count)]
    ).reshape(2, band_count, band_devices, cell_count // band_devices)
    moved = lax.all_to_all(both, "band", 2, 1, tiled=True)
    bands_here = moved[0].reshape(total_bands, -1)
    image_here = moved[1].reshape(total_bands, -1)
    margin_part = jnp.dot(
        bands_here,
        bands_here.T,
        precision=lax.Precision.HIGHEST,
        preferred_element_type=jnp.float32,
    )
    image_part = jnp.dot(
        image_here,
        bands_here.T,
        precision=lax.Precision.HIGHEST,
        preferred_element_type=jnp.float32,
    )
    norm_part = jnp.sum(image_here * image_here, axis=1)
    packed = jnp.concatenate([margin_part.reshape(-1), image_part.reshape(-1), norm_part])
    packed = lax.psum(packed, ("band", "grid")) * inverse_cells
    square = total_bands * total_bands
    margin = packed[:square].reshape(total_bands, total_bands)
    subspace = packed[square : 2 * square].reshape(total_bands, total_bands)
    image_norms = packed[2 * square :]
    factor = jnp.linalg.cholesky(margin)
    coefficients = lax.linalg.triangular_solve(factor, subspace.T, left_side=True, lower=True)
    projected = lax.linalg.triangular_solve(factor, coefficients.T, left_side=True, lower=True)
    residual_norms = image_norms - jnp.sum(coefficients * coefficients, axis=0)
    projected_rows = lax.dynamic_slice_in_dim(projected, first_band, band_count, 0)
    residual_rows = lax.dynamic_slice_in_dim(residual_norms, first_band, band_count, 0)
    return (current, projected_rows, residual_rows)


def solution(mesh):
    in_specs = (P("band", "grid", None, None), P("grid", None, None))
    out_specs = (P("band", "grid", None, None), P("band", None), P("band"))
    return jax.shard_map(
        on_device, mesh=mesh, in_specs=in_specs, out_specs=out_specs, check_vma=False
    )
```

profile of v0, /device:TPU:1, one launch (start us, length us, event | category | flops | bytes accessed | tf_op | source)
XLA Modules:
  0.0 275.6 jit_solution(5035472801133282586)
XLA Ops:
  0.6 0.9 fusion.146
  1.5 4.6 %collective-permute-start = (f32[2,2,32,128]{3,2,1,0:T(8,128)S(1)}, f32[2,2,32,128]{3,2,1,0:T(8,128)S(1)}, u32[]{:S(2)}, u32[]{:S(2)}) collective-permute-start(f32[2,2,32,128]{3,2,1,0:T(8,128)S(1)} %get-tuple-element.91), channel_id=1, source_target_pairs={{0,1},{1,2},{2,3},{3,4},{4,5},{5,6},{6,7},{7,8},{8,9},{9,10},{10,1... | collective-permute-start | bytes 196616 | tf_op jit(solution)/shard_map/ppermute | solution.py:22
  6.1 6.2 %collective-permute-start.1 = (f32[2,2,32,128]{3,2,1,0:T(8,128)S(1)}, f32[2,2,32,128]{3,2,1,0:T(8,128)S(1)}, u32[]{:S(2)}, u32[]{:S(2)}) collective-permute-start(f32[2,2,32,128]{3,2,1,0:T(8,128)S(1)} %get-tuple-element.92), channel_id=1, source_target_pairs={{1,0},{2,1},{3,2},{4,3},{5,4},{6,5},{7,6},{8,7},{9,8},{10,9},{11,1... | collective-permute-start | bytes 196616 | tf_op jit(solution)/shard_map/ppermute | solution.py:24
  12.4 1.2 fusion.150
  14.3 0.7 copy-done.2
  15.2 0.7 broadcast_multiply_fusion
  16.7 1.9 collective-permute-start.2
  18.6 14.5 %collective-permute-start.3 = (f32[2,2,32,128]{3,2,1,0:T(8,128)S(1)}, f32[2,2,32,128]{3,2,1,0:T(8,128)S(1)}, u32[]{:S(2)}, u32[]{:S(2)}) collective-permute-start(f32[2,2,32,128]{3,2,1,0:T(8,128)S(1)} %get-tuple-element.80), channel_id=1, source_target_pairs={{1,0},{2,1},{3,2},{4,3},{5,4},{6,5},{7,6},{8,7},{9,8},{10,9},{11,1... | collective-permute-start | bytes 196616 | tf_op jit(solution)/shard_map/ppermute | solution.py:24
  33.1 0.8 collective-permute-done.3
  34.0 0.7 fusion.55
  35.5 1.9 collective-permute-start.4
  37.4 15.5 %collective-permute-start.5 = (f32[2,2,32,128]{3,2,1,0:T(8,128)S(1)}, f32[2,2,32,128]{3,2,1,0:T(8,128)S(1)}, u32[]{:S(2)}, u32[]{:S(2)}) collective-permute-start(f32[2,2,32,128]{3,2,1,0:T(8,128)S(1)} %get-tuple-element.62), channel_id=1, source_target_pairs={{1,0},{2,1},{3,2},{4,3},{5,4},{6,5},{7,6},{8,7},{9,8},{10,9},{11,1... | collective-permute-start | bytes 196616 | tf_op jit(solution)/shard_map/ppermute | solution.py:24
  52.9 0.8 collective-permute-done.5
  55.2 1.9 collective-permute-start.6
  57.2 15.5 %collective-permute-start.7 = (f32[2,2,32,128]{3,2,1,0:T(8,128)S(1)}, f32[2,2,32,128]{3,2,1,0:T(8,128)S(1)}, u32[]{:S(2)}, u32[]{:S(2)}) collective-permute-start(f32[2,2,32,128]{3,2,1,0:T(8,128)S(1)} %get-tuple-element.44), channel_id=1, source_target_pairs={{1,0},{2,1},{3,2},{4,3},{5,4},{6,5},{7,6},{8,7},{9,8},{10,9},{11,1... | collective-permute-start | bytes 196616 | tf_op jit(solution)/shard_map/ppermute | solution.py:24
  72.7 0.8 collective-permute-done.7
  74.8 0.9 fusion.111
  75.7 0.9 fusion.112
  76.6 0.7 fusion.114
  77.3 1.9 collective-permute-start.8
  79.2 15.5 %collective-permute-start.9 = (f32[2,2,32,128]{3,2,1,0:T(8,128)}, f32[2,2,32,128]{3,2,1,0:T(8,128)}, u32[]{:S(2)}, u32[]{:S(2)}) collective-permute-start(f32[2,2,32,128]{3,2,1,0:T(8,128)} %get-tuple-element.26), channel_id=1, source_target_pairs={{1,0},{2,1},{3,2},{4,3},{5,4},{6,5},{7,6},{8,7},{9,8},{10,9},{11,1... | collective-permute-start | bytes 196616 | tf_op jit(solution)/shard_map/ppermute | solution.py:24
  95.4 0.8 stack.7
  96.2 0.7 copy-done.4
  96.9 2.5 fusion.10
  99.4 1.1 stack.8
  100.5 1.4 copy.10
  101.9 10.4 %all-to-all-start = ((f32[2,2,32,1280]{3,1,0,2:T(2,128)}), f32[2,2,32,1280]{3,1,0,2:T(2,128)S(1)}, u32[]{:S(2)}, u32[]{:S(2)}) async-start(f32[2,2,32,1280]{3,1,0,2:T(2,128)} %copy.10), calls=%async_computation | async-start | bytes 1310720 | tf_op jit(solution)/shard_map/all_to_all | solution.py:65
  112.3 22.4 %all-to-all-done = f32[2,2,32,1280]{3,1,0,2:T(2,128)S(1)} async-done(((f32[2,2,32,1280]{3,1,0,2:T(2,128)}), f32[2,2,32,1280]{3,1,0,2:T(2,128)S(1)}, u32[]{:S(2)}, u32[]{:S(2)}) %all-to-all-start) | async-done | bytes 655392 | tf_op jit(solution)/shard_map/all_to_all | solution.py:65
  136.5 125.1 %psum.7 = f32[8256]{0:T(1024)S(1)} all-reduce(f32[8256]{0:T(1024)S(1)} %pad_maximum_fusion.9), channel_id=1, replica_groups=mesh['band'=32,'grid'=16] {'band','grid'}, use_global_device_ids=true, to_apply=%region_1.2 | all-reduce | flops 8256 | bytes 66048 | tf_op jit(solution)/shard_map/psum | solution.py:82
  261.8 5.8 %cholesky.18 = f32[64,64]{1,0:T(8,128)S(1)} custom-call(f32[64,64]{1,0:T(8,128)S(1)} %fusion.103), custom_call_target="Cholesky" | custom-call | tf_op jit(solution)/shard_map/jit(cholesky)/cholesky | solution.py:87
  268.3 0.7 fusion.96
  269.0 4.9 %custom-call.8 = f32[1,64,64]{1,2,0:T(8,128)S(1)} custom-call(f32[1,64,64]{2,1,0:T(8,128)S(1)} %fusion.96), custom_call_target="InvertDiagBlocksLowerTriangular" | custom-call | tf_op jit(solution)/shard_map/triangular_solve/custom-call.0 | solution.py:89
  (86 shorter events, 10.1 us)
Async XLA Ops:
  1.5 13.5 %collective-permute-start = (f32[2,2,32,128]{3,2,1,0:T(8,128)S(1)}, f32[2,2,32,128]{3,2,1,0:T(8,128)S(1)}, u32[]{:S(2)}, u32[]{:S(2)}) collective-permute-start(f32[2,2,32,128]{3,2,1,0:T(8,128)S(1)} %get-tuple-element.91), channel_id=1, source_target_pairs={{0,1},{1,2},{2,3},{3,4},{4,5},{5,6},{6,7},{7,8},{8,9},{9,10},{10,1... | collective-permute-start | bytes 196616 | tf_op jit(solution)/shard_map/ppermute | solution.py:22
  6.1 7.5 %copy-start.1 = (f32[2,10,32,128]{3,2,1,0:T(8,128)S(1)}, f32[2,10,32,128]{3,2,1,0:T(8,128)}, u32[]{:S(2)}) copy-start(f32[2,10,32,128]{3,2,1,0:T(8,128)} %param.4) | copy-start | bytes 983044
  6.1 9.0 %collective-permute-start.1 = (f32[2,2,32,128]{3,2,1,0:T(8,128)S(1)}, f32[2,2,32,128]{3,2,1,0:T(8,128)S(1)}, u32[]{:S(2)}, u32[]{:S(2)}) collective-permute-start(f32[2,2,32,128]{3,2,1,0:T(8,128)S(1)} %get-tuple-element.92), channel_id=1, source_target_pairs={{1,0},{2,1},{3,2},{4,3},{5,4},{6,5},{7,6},{8,7},{9,8},{10,9},{11,1... | collective-permute-start | bytes 196616 | tf_op jit(solution)/shard_map/ppermute | solution.py:24
  14.1 0.9 copy-start.2
  16.7 16.4 %collective-permute-start.2 = (f32[2,2,32,128]{3,2,1,0:T(8,128)S(1)}, f32[2,2,32,128]{3,2,1,0:T(8,128)S(1)}, u32[]{:S(2)}, u32[]{:S(2)}) collective-permute-start(f32[2,2,32,128]{3,2,1,0:T(8,128)S(1)} %get-tuple-element.79), channel_id=1, source_target_pairs={{0,1},{1,2},{2,3},{3,4},{4,5},{5,6},{6,7},{7,8},{8,9},{9,10},{10,1... | collective-permute-start | bytes 196616 | tf_op jit(solution)/shard_map/ppermute | solution.py:22
  18.6 15.4 %collective-permute-start.3 = (f32[2,2,32,128]{3,2,1,0:T(8,128)S(1)}, f32[2,2,32,128]{3,2,1,0:T(8,128)S(1)}, u32[]{:S(2)}, u32[]{:S(2)}) collective-permute-start(f32[2,2,32,128]{3,2,1,0:T(8,128)S(1)} %get-tuple-element.80), channel_id=1, source_target_pairs={{1,0},{2,1},{3,2},{4,3},{5,4},{6,5},{7,6},{8,7},{9,8},{10,9},{11,1... | collective-permute-start | bytes 196616 | tf_op jit(solution)/shard_map/ppermute | solution.py:24
  35.5 17.4 %collective-permute-start.4 = (f32[2,2,32,128]{3,2,1,0:T(8,128)S(1)}, f32[2,2,32,128]{3,2,1,0:T(8,128)S(1)}, u32[]{:S(2)}, u32[]{:S(2)}) collective-permute-start(f32[2,2,32,128]{3,2,1,0:T(8,128)S(1)} %get-tuple-element.61), channel_id=1, source_target_pairs={{0,1},{1,2},{2,3},{3,4},{4,5},{5,6},{6,7},{7,8},{8,9},{9,10},{10,1... | collective-permute-start | bytes 196616 | tf_op jit(solution)/shard_map/ppermute | solution.py:22
  37.4 16.4 %collective-permute-start.5 = (f32[2,2,32,128]{3,2,1,0:T(8,128)S(1)}, f32[2,2,32,128]{3,2,1,0:T(8,128)S(1)}, u32[]{:S(2)}, u32[]{:S(2)}) collective-permute-start(f32[2,2,32,128]{3,2,1,0:T(8,128)S(1)} %get-tuple-element.62), channel_id=1, source_target_pairs={{1,0},{2,1},{3,2},{4,3},{5,4},{6,5},{7,6},{8,7},{9,8},{10,9},{11,1... | collective-permute-start | bytes 196616 | tf_op jit(solution)/shard_map/ppermute | solution.py:24
  55.2 17.5 %collective-permute-start.6 = (f32[2,2,32,128]{3,2,1,0:T(8,128)S(1)}, f32[2,2,32,128]{3,2,1,0:T(8,128)S(1)}, u32[]{:S(2)}, u32[]{:S(2)}) collective-permute-start(f32[2,2,32,128]{3,2,1,0:T(8,128)S(1)} %get-tuple-element.43), channel_id=1, source_target_pairs={{0,1},{1,2},{2,3},{3,4},{4,5},{5,6},{6,7},{7,8},{8,9},{9,10},{10,1... | collective-permute-start | bytes 196616 | tf_op jit(solution)/shard_map/ppermute | solution.py:22
  57.2 16.4 %collective-permute-start.7 = (f32[2,2,32,128]{3,2,1,0:T(8,128)S(1)}, f32[2,2,32,128]{3,2,1,0:T(8,128)S(1)}, u32[]{:S(2)}, u32[]{:S(2)}) collective-permute-start(f32[2,2,32,128]{3,2,1,0:T(8,128)S(1)} %get-tuple-element.44), channel_id=1, source_target_pairs={{1,0},{2,1},{3,2},{4,3},{5,4},{6,5},{7,6},{8,7},{9,8},{10,9},{11,1... | collective-permute-start | bytes 196616 | tf_op jit(solution)/shard_map/ppermute | solution.py:24
  74.2 21.9 %copy-start = (f32[2,10,32,128]{3,2,1,0:T(8,128)}, f32[2,10,32,128]{3,2,1,0:T(8,128)S(1)}, u32[]{:S(2)}) copy-start(f32[2,10,32,128]{3,2,1,0:T(8,128)S(1)} %fusion.25) | copy-start | bytes 983044
  77.3 18.9 %collective-permute-start.8 = (f32[2,2,32,128]{3,2,1,0:T(8,128)}, f32[2,2,32,128]{3,2,1,0:T(8,128)S(1)}, u32[]{:S(2)}, u32[]{:S(2)}) collective-permute-start(f32[2,2,32,128]{3,2,1,0:T(8,128)} %get-tuple-element.25), channel_id=1, source_target_pairs={{0,1},{1,2},{2,3},{3,4},{4,5},{5,6},{6,7},{7,8},{8,9},{9,10},{10,1... | collective-permute-start | bytes 196616 | tf_op jit(solution)/shard_map/ppermute | solution.py:22
  79.2 16.9 %collective-permute-start.9 = (f32[2,2,32,128]{3,2,1,0:T(8,128)}, f32[2,2,32,128]{3,2,1,0:T(8,128)}, u32[]{:S(2)}, u32[]{:S(2)}) collective-permute-start(f32[2,2,32,128]{3,2,1,0:T(8,128)} %get-tuple-element.26), channel_id=1, source_target_pairs={{1,0},{2,1},{3,2},{4,3},{5,4},{6,5},{7,6},{8,7},{9,8},{10,9},{11,1... | collective-permute-start | bytes 196616 | tf_op jit(solution)/shard_map/ppermute | solution.py:24
  96.1 0.7 copy-start.4
  96.1 0.7 copy-start.5
  99.4 1.1 copy-start.3
  101.9 32.8 %all-to-all-start = ((f32[2,2,32,1280]{3,1,0,2:T(2,128)}), f32[2,2,32,1280]{3,1,0,2:T(2,128)S(1)}, u32[]{:S(2)}, u32[]{:S(2)}) async-start(f32[2,2,32,1280]{3,1,0,2:T(2,128)} %copy.10), calls=%async_computation | async-start | bytes 1310720 | tf_op jit(solution)/shard_map/all_to_all | solution.py:65
where the time goes:
time: 276 us
  blocking collectives  125 us (45%)
  starting transfers between devices  89.9 us (33%)
  waiting for transfers between devices  25 us (9%)
  other arithmetic  17.6 us (6%)
  local copies, waits for them, and re-layouts  15.7 us (6%)
    psum x1, blocking collectives, on_device(): packed = lax.psum(packed, ('band', 'grid')) * inverse_cells  125 us
    ppermute x5, starting transfers between devices, padded_2(): lax.ppermute(head, axis, [((i + 1) % count, i) for i in range(count)])  67.2 us
    all_to_all x1, waiting for transfers between devices, on_device(): moved = lax.all_to_all(both, 'band', 2, 1, tiled=True)  22.4 us
    ppermute x5, starting transfers between devices, padded_2(): lax.ppermute(tail, axis, [(i, (i + 1) % count) for i in range(count)])  12.3 us
    all_to_all x1, starting transfers between devices, on_device(): moved = lax.all_to_all(both, 'band', 2, 1, tiled=True)  10.4 us
    another operation x3, other arithmetic, on_device(): factor = jnp.linalg.cholesky(margin)  6.52 us
    another operation x2, other arithmetic, on_device(): lax.linalg.triangular_solve(factor, coefficients.T, left_side=True, lower...  5.55 us
  transfers between devices with their start and end apart: 11, of which 4 were waited for; matrix products, arithmetic and copies ran while one was open for 1% of the time, Pallas kernels for 0%

commit v1 on v0

--- a/solution.py
+++ b/solution.py
@@ -79,7 +79,7 @@
     )
     norm_part = jnp.sum(image_here * image_here, axis=1)
     packed = jnp.concatenate([margin_part.reshape(-1), image_part.reshape(-1), norm_part])
-    packed = lax.psum(packed, ("band", "grid")) * inverse_cells
+    packed = jnp.sum(lax.all_gather(packed, ("band", "grid")), axis=0) * inverse_cells
     square = total_bands * total_bands
     margin = packed[:square].reshape(total_bands, total_bands)
     subspace = packed[square : 2 * square].reshape(total_bands, total_bands)

time: 276 us -> 750 us (2.72)
  waiting for transfers between devices: 25 us -> 566 us
  blocking collectives: 125 us -> 0 us
  local copies, waits for them, and re-layouts: 15.7 us -> 47.8 us
  between operations: 1.13 us -> 14.5 us
  other arithmetic: 17.6 us -> 28.6 us
    unnamed x0 -> x2, waiting for transfers between devices: none -> 541 us
    psum x1 -> x0, blocking collectives: 125 us -> none  [on_device(): packed = lax.psum(packed, ('band', 'grid')) * inverse_cells]
    all_gather x0 -> x1, local copies, waits for them, and re-layouts: none -> 19.3 us  [on_device(): lax.all_gather(packed, ('band', 'grid'))]
  transfers between devices with their start and end apart: 11 -> 12, of which waited for: 4 -> 5; matrix products, arithmetic and copies ran while one was open for 1% -> 2% of each run, Pallas kernels for 0% -> 0%
where the time goes in v1:
time: 750 us; the launch traced here: 748 us
  waiting for transfers between devices  566 us (75%)
  starting transfers between devices  90 us (12%)
  local copies, waits for them, and re-layouts  47.8 us (6%)
  other arithmetic  28.6 us (4%)
  between operations  14.5 us (2%)
    unnamed x2, waiting for transfers between devices  541 us
    ppermute x5, starting transfers between devices, padded_2(): lax.ppermute(head, axis, [((i + 1) % count, i) for i in range(count)])  67.1 us
    all_to_all x1, waiting for transfers between devices, on_device(): moved = lax.all_to_all(both, 'band', 2, 1, tiled=True)  22.2 us
    all_gather x1, local copies, waits for them, and re-layouts, on_device(): lax.all_gather(packed, ('band', 'grid'))  19.3 us
  transfers between devices with their start and end apart: 12, of which 5 were waited for; matrix products, arithmetic and copies ran while one was open for 2% of the time, Pallas kernels for 0%

profile of v1, /device:TPU:1, one launch (start us, length us, event | category | flops | bytes accessed | tf_op | source)
XLA Modules:
  0.0 747.9 jit_solution(6072653588970547377)
XLA Ops:
  8.1 4.6 collective-permute-start
  12.7 6.1 collective-permute-start.1
  19.8 1.2 fusion.144
  21.0 1.1 fusion.148
  22.2 1.1 fusion.143
  23.3 1.3 fusion.149
  24.6 1.2 fusion.145
  25.8 1.2 fusion.150
  28.9 1.0 constant_dynamic-update-slice_fusion
  30.0 1.7 broadcast_multiply_fusion
  32.5 1.9 collective-permute-start.2
  34.5 14.5 %collective-permute-start.3 = (f32[2,2,32,128]{3,2,1,0:T(8,128)S(1)}, f32[2,2,32,128]{3,2,1,0:T(8,128)S(1)}, u32[]{:S(2)}, u32[]{:S(2)}) collective-permute-start(f32[2,2,32,128]{3,2,1,0:T(8,128)S(1)} %get-tuple-element.80), channel_id=1, source_target_pairs={{1,0},{2,1},{3,2},{4,3},{5,4},{6,5},{7,6},{8,7},{9,8},{10,9},{11,1... | collective-permute-start | bytes 196616 | tf_op jit(solution)/shard_map/ppermute | solution.py:24
  51.3 1.9 collective-permute-start.4
  53.3 15.5 %collective-permute-start.5 = (f32[2,2,32,128]{3,2,1,0:T(8,128)S(1)}, f32[2,2,32,128]{3,2,1,0:T(8,128)S(1)}, u32[]{:S(2)}, u32[]{:S(2)}) collective-permute-start(f32[2,2,32,128]{3,2,1,0:T(8,128)S(1)} %get-tuple-element.62), channel_id=1, source_target_pairs={{1,0},{2,1},{3,2},{4,3},{5,4},{6,5},{7,6},{8,7},{9,8},{10,9},{11,1... | collective-permute-start | bytes 196616 | tf_op jit(solution)/shard_map/ppermute | solution.py:24
  71.1 1.9 collective-permute-start.6
  73.0 15.5 %collective-permute-start.7 = (f32[2,2,32,128]{3,2,1,0:T(8,128)S(1)}, f32[2,2,32,128]{3,2,1,0:T(8,128)S(1)}, u32[]{:S(2)}, u32[]{:S(2)}) collective-permute-start(f32[2,2,32,128]{3,2,1,0:T(8,128)S(1)} %get-tuple-element.44), channel_id=1, source_target_pairs={{1,0},{2,1},{3,2},{4,3},{5,4},{6,5},{7,6},{8,7},{9,8},{10,9},{11,1... | collective-permute-start | bytes 196616 | tf_op jit(solution)/shard_map/ppermute | solution.py:24
  92.2 1.0 fusion.107
  93.1 1.9 collective-permute-start.8
  95.1 15.5 %collective-permute-start.9 = (f32[2,2,32,128]{3,2,1,0:T(8,128)}, f32[2,2,32,128]{3,2,1,0:T(8,128)}, u32[]{:S(2)}, u32[]{:S(2)}) collective-permute-start(f32[2,2,32,128]{3,2,1,0:T(8,128)} %get-tuple-element.26), channel_id=1, source_target_pairs={{1,0},{2,1},{3,2},{4,3},{5,4},{6,5},{7,6},{8,7},{9,8},{10,9},{11,1... | collective-permute-start | bytes 196616 | tf_op jit(solution)/shard_map/ppermute | solution.py:24
  112.0 2.5 fusion.10
  114.5 1.0 stack.8
  115.6 1.0 pad_maximum_fusion
  116.6 1.4 copy.10
  118.0 10.4 %all-to-all-start = ((f32[2,2,32,1280]{3,1,0,2:T(2,128)}), f32[2,2,32,1280]{3,1,0,2:T(2,128)S(1)}, u32[]{:S(2)}, u32[]{:S(2)}) async-start(f32[2,2,32,1280]{3,1,0,2:T(2,128)} %copy.10), calls=%async_computation | async-start | bytes 1310720 | tf_op jit(solution)/shard_map/all_to_all | solution.py:65
  128.6 22.2 %all-to-all-done = f32[2,2,32,1280]{3,1,0,2:T(2,128)S(1)} async-done(((f32[2,2,32,1280]{3,1,0,2:T(2,128)}), f32[2,2,32,1280]{3,1,0,2:T(2,128)S(1)}, u32[]{:S(2)}, u32[]{:S(2)}) %all-to-all-start) | async-done | bytes 655392 | tf_op jit(solution)/shard_map/all_to_all | solution.py:65
  152.6 6.0 broadcast.74
  158.7 1.5 maximum_dynamic-update-slice_fusion
  160.2 540.9 %all-reduce.3.cloned.1.call-done = f32[4227072]{0:T(1024)} async-done(((f32[4227072]{0:T(1024)}), f32[4227072]{0:T(1024)}) %all-reduce.3.cloned.1.call-update) | async-done | bytes 16908304
  701.1 19.3 %reshape.49 = f32[512,8256]{1,0:T(8,128)} reshape(f32[4227072]{0:T(1024)} %all-reduce.3.cloned.1.call-done) | data formatting | bytes 33816576 | tf_op jit(solution)/shard_map/all_gather | solution.py:82
  720.4 6.6 reduce_sum.31
  727.2 5.8 cholesky.18
  734.4 4.9 custom-call.8
  (85 shorter events, 19.5 us)
Async XLA Ops:
  7.2 42.7 %copy-start.1 = (f32[2,10,32,128]{3,2,1,0:T(8,128)S(1)}, f32[2,10,32,128]{3,2,1,0:T(8,128)}, u32[]{:S(2)}) copy-start(f32[2,10,32,128]{3,2,1,0:T(8,128)} %param.4) | copy-start | bytes 983044
  8.1 20.8 %collective-permute-start = (f32[2,2,32,128]{3,2,1,0:T(8,128)S(1)}, f32[2,2,32,128]{3,2,1,0:T(8,128)S(1)}, u32[]{:S(2)}, u32[]{:S(2)}) collective-permute-start(f32[2,2,32,128]{3,2,1,0:T(8,128)S(1)} %get-tuple-element.91), channel_id=1, source_target_pairs={{0,1},{1,2},{2,3},{3,4},{4,5},{5,6},{6,7},{7,8},{8,9},{9,10},{10,1... | collective-permute-start | bytes 196616 | tf_op jit(solution)/shard_map/ppermute | solution.py:22
  12.7 17.3 %collective-permute-start.1 = (f32[2,2,32,128]{3,2,1,0:T(8,128)S(1)}, f32[2,2,32,128]{3,2,1,0:T(8,128)S(1)}, u32[]{:S(2)}, u32[]{:S(2)}) collective-permute-start(f32[2,2,32,128]{3,2,1,0:T(8,128)S(1)} %get-tuple-element.92), channel_id=1, source_target_pairs={{1,0},{2,1},{3,2},{4,3},{5,4},{6,5},{7,6},{8,7},{9,8},{10,9},{11,1... | collective-permute-start | bytes 196616 | tf_op jit(solution)/shard_map/ppermute | solution.py:24
  23.3 46.3 %copy-start.2 = (f32[10,32,128]{2,1,0:T(8,128)S(1)}, f32[10,32,128]{2,1,0:T(8,128)}, u32[]{:S(2)}) copy-start(f32[10,32,128]{2,1,0:T(8,128)} %param.5) | copy-start | bytes 491524
  32.5 16.4 %collective-permute-start.2 = (f32[2,2,32,128]{3,2,1,0:T(8,128)S(1)}, f32[2,2,32,128]{3,2,1,0:T(8,128)S(1)}, u32[]{:S(2)}, u32[]{:S(2)}) collective-permute-start(f32[2,2,32,128]{3,2,1,0:T(8,128)S(1)} %get-tuple-element.79), channel_id=1, source_target_pairs={{0,1},{1,2},{2,3},{3,4},{4,5},{5,6},{6,7},{7,8},{8,9},{9,10},{10,1... | collective-permute-start | bytes 196616 | tf_op jit(solution)/shard_map/ppermute | solution.py:22
  34.5 15.4 %collective-permute-start.3 = (f32[2,2,32,128]{3,2,1,0:T(8,128)S(1)}, f32[2,2,32,128]{3,2,1,0:T(8,128)S(1)}, u32[]{:S(2)}, u32[]{:S(2)}) collective-permute-start(f32[2,2,32,128]{3,2,1,0:T(8,128)S(1)} %get-tuple-element.80), channel_id=1, source_target_pairs={{1,0},{2,1},{3,2},{4,3},{5,4},{6,5},{7,6},{8,7},{9,8},{10,9},{11,1... | collective-permute-start | bytes 196616 | tf_op jit(solution)/shard_map/ppermute | solution.py:24
  51.3 17.4 %collective-permute-start.4 = (f32[2,2,32,128]{3,2,1,0:T(8,128)S(1)}, f32[2,2,32,128]{3,2,1,0:T(8,128)S(1)}, u32[]{:S(2)}, u32[]{:S(2)}) collective-permute-start(f32[2,2,32,128]{3,2,1,0:T(8,128)S(1)} %get-tuple-element.61), channel_id=1, source_target_pairs={{0,1},{1,2},{2,3},{3,4},{4,5},{5,6},{6,7},{7,8},{8,9},{9,10},{10,1... | collective-permute-start | bytes 196616 | tf_op jit(solution)/shard_map/ppermute | solution.py:22
  53.3 16.4 %collective-permute-start.5 = (f32[2,2,32,128]{3,2,1,0:T(8,128)S(1)}, f32[2,2,32,128]{3,2,1,0:T(8,128)S(1)}, u32[]{:S(2)}, u32[]{:S(2)}) collective-permute-start(f32[2,2,32,128]{3,2,1,0:T(8,128)S(1)} %get-tuple-element.62), channel_id=1, source_target_pairs={{1,0},{2,1},{3,2},{4,3},{5,4},{6,5},{7,6},{8,7},{9,8},{10,9},{11,1... | collective-permute-start | bytes 196616 | tf_op jit(solution)/shard_map/ppermute | solution.py:24
  71.1 17.5 %collective-permute-start.6 = (f32[2,2,32,128]{3,2,1,0:T(8,128)S(1)}, f32[2,2,32,128]{3,2,1,0:T(8,128)S(1)}, u32[]{:S(2)}, u32[]{:S(2)}) collective-permute-start(f32[2,2,32,128]{3,2,1,0:T(8,128)S(1)} %get-tuple-element.43), channel_id=1, source_target_pairs={{0,1},{1,2},{2,3},{3,4},{4,5},{5,6},{6,7},{7,8},{8,9},{9,10},{10,1... | collective-permute-start | bytes 196616 | tf_op jit(solution)/shard_map/ppermute | solution.py:22
  73.0 16.4 %collective-permute-start.7 = (f32[2,2,32,128]{3,2,1,0:T(8,128)S(1)}, f32[2,2,32,128]{3,2,1,0:T(8,128)S(1)}, u32[]{:S(2)}, u32[]{:S(2)}) collective-permute-start(f32[2,2,32,128]{3,2,1,0:T(8,128)S(1)} %get-tuple-element.44), channel_id=1, source_target_pairs={{1,0},{2,1},{3,2},{4,3},{5,4},{6,5},{7,6},{8,7},{9,8},{10,9},{11,1... | collective-permute-start | bytes 196616 | tf_op jit(solution)/shard_map/ppermute | solution.py:24
  90.1 68.6 %copy-start = (f32[2,10,32,128]{3,2,1,0:T(8,128)}, f32[2,10,32,128]{3,2,1,0:T(8,128)S(1)}, u32[]{:S(2)}) copy-start(f32[2,10,32,128]{3,2,1,0:T(8,128)S(1)} %fusion.25) | copy-start | bytes 983044
  93.1 18.9 %collective-permute-start.8 = (f32[2,2,32,128]{3,2,1,0:T(8,128)}, f32[2,2,32,128]{3,2,1,0:T(8,128)S(1)}, u32[]{:S(2)}, u32[]{:S(2)}) collective-permute-start(f32[2,2,32,128]{3,2,1,0:T(8,128)} %get-tuple-element.25), channel_id=1, source_target_pairs={{0,1},{1,2},{2,3},{3,4},{4,5},{5,6},{6,7},{7,8},{8,9},{9,10},{10,1... | collective-permute-start | bytes 196616 | tf_op jit(solution)/shard_map/ppermute | solution.py:22
  95.1 16.9 %collective-permute-start.9 = (f32[2,2,32,128]{3,2,1,0:T(8,128)}, f32[2,2,32,128]{3,2,1,0:T(8,128)}, u32[]{:S(2)}, u32[]{:S(2)}) collective-permute-start(f32[2,2,32,128]{3,2,1,0:T(8,128)} %get-tuple-element.26), channel_id=1, source_target_pairs={{1,0},{2,1},{3,2},{4,3},{5,4},{6,5},{7,6},{8,7},{9,8},{10,9},{11,1... | collective-permute-start | bytes 196616 | tf_op jit(solution)/shard_map/ppermute | solution.py:24
  118.0 32.8 %all-to-all-start = ((f32[2,2,32,1280]{3,1,0,2:T(2,128)}), f32[2,2,32,1280]{3,1,0,2:T(2,128)S(1)}, u32[]{:S(2)}, u32[]{:S(2)}) async-start(f32[2,2,32,1280]{3,1,0,2:T(2,128)} %copy.10), calls=%async_computation | async-start | bytes 1310720 | tf_op jit(solution)/shard_map/all_to_all | solution.py:65
  128.4 572.7 %all-reduce.3.cloned.1.call-start = ((), (), s32[]{:S(2)}) async-start(), calls=%async_computation.1 | async-start | bytes 33816576
Sparse Core Ops, SparseCore 0:
  160.3 540.7 all-reduce.2
